TPU v7x, 512 devices: a whole 4x8x8 slice. The times are simulated.
512 devices in a mesh: tm: 16 (over y_lo, x), space: 32 (over z, y_hi, core).
Axes of the slice: x: 4, y: 8 (y_hi: 2, y_lo: 4; y = y_hi * 4 + y_lo), z: 8, core: 2. Of those that a mesh axis runs over, the one named last changes fastest.
Arguments:
- frames: bfloat16 [16, 64, 96, 384], P('tm', 'space'), may hold values from -8 to 8
- cache_in: bfloat16 [2, 64, 96, 384], P(None, 'space'), may hold values from -6 to 6
- norm_gain: bfloat16 [384], replicated, may hold values from 0.5 to 1.5
- w_qkv: bfloat16 [384, 1152], replicated, may hold values from -0.5 to 0.5
- b_qkv: bfloat16 [1152], replicated, may hold values from -3 to 3
- w_proj: bfloat16 [384, 384], replicated, may hold values from -1.25 to 1.25
- b_proj: bfloat16 [384], replicated, may hold values from -2 to 2
- w_time: bfloat16 [3, 384, 768], replicated, may hold values from -0.1875 to 0.1875
- b_time: bfloat16 [768], replicated, may hold values from -3 to 3
- w_space: bfloat16 [3, 3, 384, 192], replicated, may hold values from -0.109375 to 0.109375
- b_space: bfloat16 [192], replicated, may hold values from -3 to 3
Outputs:
- decoded: bfloat16 [32, 128, 192, 192], P('tm', 'space')
All inputs are finite; a program needn't handle non-finite values.
Results may differ from a plain program's by a relative error of at most 0.01.
Values may be sent and summed in bfloat16 or wider, within the bound.
No kernel may reach another device: no remote copies, remote signals or barrier semaphores. Data moves between devices by JAX's collectives and lax.ppermute only.
A program may use at most 64 MiB of HBM per device.

v0:
```python
import jax
import jax.numpy as jnp
from jax import lax
from jax.sharding import PartitionSpec as P

EPSILON = 1e-06


def shifted(value, axis, steps):
    count = lax.axis_size(axis)
    leading, last = (max(0, -steps), min(count, count - steps))
    return lax.ppermute(value, axis, [(source, source + steps) for source in range(leading, last)])


def with_halo(block, sides, width):
    for axis, dim in sides:
        count = lax.axis_size(axis)
        forward = [(i, i + 1) for i in range(count - 1)]
        backward = [(target, source) for source, target in forward]
        low = lax.ppermute(
            lax.slice_in_dim(block, block.shape[dim] - width, None, axis=dim), axis, forward
        )
        high = lax.ppermute(lax.slice_in_dim(block, 0, width, axis=dim), axis, backward)
        block = jnp.concatenate([low, block, high], axis=dim)
    return block


def normalize(frames, norm_gain):
    widened = frames.astype(jnp.float32)
    inverse = lax.rsqrt(jnp.mean(widened * widened, axis=-1, keepdims=True) + EPSILON)
    return (widened * inverse * norm_gain.astype(jnp.float32)).astype(jnp.bfloat16)


def project(rows, weight, bias):
    return (
        jnp.dot(rows, weight, preferred_element_type=jnp.float32) + bias.astype(jnp.float32)
    ).astype(jnp.bfloat16)


def attend(running, queries, key_rows, value_rows):
    best, mass, total_sum = running
    scores = lax.dot_general(
        queries, key_rows, (((1,), (1,)), ((), ())), preferred_element_type=jnp.float32
    ) * queries.shape[1] ** (-0.5)
    new_best = jnp.maximum(best, jnp.max(scores, axis=1, keepdims=True))
    weights = jnp.exp(scores - new_best)
    mass = jnp.sum(weights, axis=1, keepdims=True)
    total_sum = jnp.dot(
        weights.astype(jnp.bfloat16), value_rows, preferred_element_type=jnp.float32
    )
    return (new_best, mass, total_sum)


def body(
    frames, cache_in, norm_gain, w_qkv, b_qkv, w_proj, b_proj, w_time, b_time, w_space, b_space
):
    channels = frames.shape[-1]
    rows = frames.shape[1]
    width = frames.shape[2]
    whole = lax.all_gather(frames.reshape(-1, channels), "space", axis=0, tiled=True)
    normed = normalize(frames, norm_gain).reshape(-1, channels)
    queries = project(normed, w_qkv[:, :channels], b_qkv[:channels])
    count = queries.shape[0]
    start_state = (
        jnp.full((count, 1), -1e30, jnp.float32),
        jnp.zeros((count, 1), jnp.float32),
        jnp.zeros((count, channels), jnp.float32),
    )
    normed_all = normalize(whole, norm_gain)
    key_rows = project(
        normed_all, w_qkv[:, channels : 2 * channels], b_qkv[channels : 2 * channels]
    )
    value_rows = project(normed_all, w_qkv[:, 2 * channels :], b_qkv[2 * channels :])
    final = attend(start_state, queries, key_rows, value_rows)
    mixed = (final[2] / final[1]).astype(jnp.bfloat16)
    hidden = (
        frames.reshape(-1, channels).astype(jnp.float32)
        + jnp.dot(mixed, w_proj, preferred_element_type=jnp.float32)
        + b_proj.astype(jnp.float32)
    ).astype(jnp.bfloat16)
    position = lax.axis_index("tm")
    carried = cache_in.reshape(2, -1, channels)
    near_frame = shifted(hidden, "tm", 1)
    near_frame = jnp.where(position == 0, carried[1], near_frame)
    far_frame = shifted(hidden, "tm", 2)
    far_frame = jnp.where(position == 1, carried[1], far_frame)
    far_frame = jnp.where(position == 0, carried[0], far_frame)
    timed = b_time.astype(jnp.float32) + jnp.dot(
        far_frame, w_time[0], preferred_element_type=jnp.float32
    )
    timed = timed + jnp.dot(near_frame, w_time[1], preferred_element_type=jnp.float32)
    timed = (timed + jnp.dot(hidden, w_time[2], preferred_element_type=jnp.float32)).astype(
        jnp.bfloat16
    )
    paired = jnp.stack([timed[:, :channels], timed[:, channels:]]).reshape(2, rows, width, channels)
    padded = with_halo(paired, (("space", 1),), 1)
    upsampled = jnp.repeat(jnp.repeat(padded, 2, axis=1)[:, 1 : 2 * rows + 3], 2, axis=2)
    upsampled = jnp.pad(upsampled, ((0, 0), (0, 0), (1, 1), (0, 0)))
    out_channels = w_space.shape[-1]
    result = jnp.zeros((8 * rows * width, out_channels), jnp.float32) + b_space.astype(jnp.float32)
    for row_tap in range(3):
        for col_tap in range(3):
            window = upsampled[
                :, row_tap : row_tap + 2 * rows, col_tap : col_tap + 2 * width
            ].reshape(-1, channels)
            result = result + jnp.dot(
                window, w_space[row_tap, col_tap], preferred_element_type=jnp.float32
            )
    return result.astype(jnp.bfloat16).reshape(2, 2 * rows, 2 * width, out_channels)


def solution(mesh):
    return jax.shard_map(
        body,
        mesh=mesh,
        in_specs=(
            P("tm", "space", None, None),
            P(None, "space", None, None),
            P(),
            P(),
            P(),
            P(),
            P(),
            P(),
            P(),
            P(),
            P(),
        ),
        out_specs=P("tm", "space", None, None),
        check_vma=False,
    )
```

profile of v0, /device:TPU:49, one launch (start us, length us, event | category | flops | bytes accessed | tf_op | source)
XLA Modules:
  0.0 203.1 jit_solution(68712272117767527)
XLA Ops:
  6.5 0.0 copy-start
  6.5 0.0 all-gather.2.cloned.1.call-start
  6.5 0.7 all-gather.2.cloned.1.call-update
  7.3 0.7 convert_element_type.67
  7.9 0.7 convert_element_type.79
  8.6 0.7 convert_element_type.64
  9.3 1.0 fusion.38
  10.3 0.8 slice_convert_fusion.1
  11.2 1.0 fusion.40
  12.2 1.0 fusion.67
  13.2 1.2 fusion.18
  14.4 108.0 %all-gather.2.cloned.1.call-done = bf16[6144,384]{1,0:T(8,128)(2,1)} async-done(((bf16[192,384]{1,0:T(8,128)(2,1)}), bf16[6144,384]{1,0:T(8,128)(2,1)}) %all-gather.2.cloned.1.call-update) | async-done | bytes 4718608 | tf_op jit(solution)/shard_map/all_gather | solution.py:60
  122.4 3.3 %fusion = f32[6144]{0:T(1024)S(1)} fusion(bf16[6144,384]{1,0:T(8,128)(2,1)} %all-gather.2.cloned.1.call-done), kind=kLoop, calls=%fused_computation.2 | loop fusion | flops 7071744 | bytes 4743168 | tf_op jit(solution)/shard_map/reduce_sum | solution.py:30
  125.8 8.1 %fusion.68 = (f32[192]{0:T(256)S(1)}, f32[192,6144]{1,0:T(8,128)}) fusion(bf16[192,384]{1,0:T(8,128)(2,1)S(1)} %fusion.18, f32[384]{0:T(512)S(1)} %get-tuple-element.22, bf16[6144,384]{1,0:T(8,128)(2,1)} %all-gather.2.cloned.1.call-done, f32[384]{0:T(512)S(1)} %convert_element_type.67, f32[6144]{0:T(1024)S(1)} %add_rsqrt_fusion, bf16[384,1152]{1,0:T(8,128)(2,1)} %param.14), kind=kOutput, calls=%fused_computation.90 | convolution fusion | flops 2734423808 | bytes 9907968 | tf_op jit(solution)/shard_map/dot_general | solution.py:42
  133.8 3.1 %fusion.3 = f32[192]{0:T(256)S(1)} fusion(f32[192,6144]{1,0:T(8,128)} %get-tuple-element.26, f32[192]{0:T(256)S(1)} %broadcast_maximum_fusion), kind=kLoop, calls=%fused_computation.9 | loop fusion | flops 2359104 | bytes 4720128 | tf_op jit(solution)/shard_map/reduce_sum | solution.py:47
  137.0 0.0 copy-start.1
  137.0 0.0 copy-start.2
  137.0 8.4 %fusion.25 = bf16[192,384]{1,0:T(8,128)(2,1)S(1)} fusion(f32[384]{0:T(512)S(1)} %get-tuple-element.24, bf16[6144,384]{1,0:T(8,128)(2,1)} %all-gather.2.cloned.1.call-done, f32[384]{0:T(512)S(1)} %convert_element_type.67, f32[6144]{0:T(1024)S(1)} %add_rsqrt_fusion, f32[192,6144]{1,0:T(8,128)} %get-tuple-element.26, f32[192]{0:T(256)S(1)} %broadcast_maximum_fusion, ...), kind=kOutput, calls=%fused_computation.33 | convolution fusion | flops 2734571520 | bytes 9908736 | tf_op jit(solution)/shard_map/dot_general | solution.py:48
  145.4 0.0 copy-done
  145.4 0.0 copy-done.1
  145.4 0.2 fusion.19
  145.7 4.6 %collective-permute-start = (bf16[192,384]{1,0:T(8,128)(2,1)S(1)}, bf16[192,384]{1,0:T(8,128)(2,1)S(1)}, u32[]{:S(2)}, u32[]{:S(2)}) collective-permute-start(bf16[192,384]{1,0:T(8,128)(2,1)S(1)} %fusion.19), channel_id=1, source_target_pairs={{0,64},{32,96},{64,128},{96,160},{128,192},{160,224},{192,256},{22... | collective-permute-start | bytes 442376 | tf_op jit(solution)/shard_map/ppermute | solution.py:12
  150.3 2.2 %collective-permute-start.1 = (bf16[192,384]{1,0:T(8,128)(2,1)S(1)}, bf16[192,384]{1,0:T(8,128)(2,1)S(1)}, u32[]{:S(2)}, u32[]{:S(2)}) collective-permute-start(bf16[192,384]{1,0:T(8,128)(2,1)S(1)} %fusion.19), channel_id=1, source_target_pairs={{0,32},{32,64},{64,96},{96,128},{128,160},{160,192},{192,224},{224... | collective-permute-start | bytes 442376 | tf_op jit(solution)/shard_map/ppermute | solution.py:12
  152.5 0.0 copy-done.2
  152.5 0.3 fusion.30
  152.8 2.3 %collective-permute-done = bf16[192,384]{1,0:T(8,128)(2,1)S(1)} collective-permute-done((bf16[192,384]{1,0:T(8,128)(2,1)S(1)}, bf16[192,384]{1,0:T(8,128)(2,1)S(1)}, u32[]{:S(2)}, u32[]{:S(2)}) %collective-permute-start) | collective-permute-done | bytes 147488 | tf_op jit(solution)/shard_map/ppermute | solution.py:12
  155.1 4.0 %collective-permute-done.1 = bf16[192,384]{1,0:T(8,128)(2,1)S(1)} collective-permute-done((bf16[192,384]{1,0:T(8,128)(2,1)S(1)}, bf16[192,384]{1,0:T(8,128)(2,1)S(1)}, u32[]{:S(2)}, u32[]{:S(2)}) %collective-permute-start.1) | collective-permute-done | bytes 147488 | tf_op jit(solution)/shard_map/ppermute | solution.py:12
  159.1 0.1 fusion.56
  159.2 0.3 fusion.32
  159.5 0.0 copy-start.4
  159.5 0.3 fusion.16
  159.9 6.8 %collective-permute-start.2 = (bf16[2,1,96,384]{3,2,1,0:T(8,128)(2,1)S(1)}, bf16[2,1,96,384]{3,2,1,0:T(8,128)(2,1)S(1)}, u32[]{:S(2)}, u32[]{:S(2)}) collective-permute-start(bf16[2,1,96,384]{3,2,1,0:T(8,128)(2,1)S(1)} %get-tuple-element.14), channel_id=1, source_target_pairs={{0,1},{1,2},{2,3},{3,4},{4,5},{5,6},{6,7},{7,8},{8,9},{9,10},{10,1... | collective-permute-start | bytes 442376 | tf_op jit(solution)/shard_map/ppermute | solution.py:20
  166.7 2.1 %collective-permute-start.3 = (bf16[2,1,96,384]{3,2,1,0:T(8,128)(2,1)S(1)}, bf16[2,1,96,384]{3,2,1,0:T(8,128)(2,1)S(1)}, u32[]{:S(2)}, u32[]{:S(2)}) collective-permute-start(bf16[2,1,96,384]{3,2,1,0:T(8,128)(2,1)S(1)} %get-tuple-element.15), channel_id=1, source_target_pairs={{1,0},{2,1},{3,2},{4,3},{5,4},{6,5},{7,6},{8,7},{9,8},{10,9},{11,1... | collective-permute-start | bytes 442376 | tf_op jit(solution)/shard_map/ppermute | solution.py:23
  168.8 0.0 copy-done.4
  168.9 1.6 collective-permute-done.2
  170.4 8.7 %collective-permute-done.3 = bf16[2,1,96,384]{3,2,1,0:T(8,128)(2,1)S(1)} collective-permute-done((bf16[2,1,96,384]{3,2,1,0:T(8,128)(2,1)S(1)}, bf16[2,1,96,384]{3,2,1,0:T(8,128)(2,1)S(1)}, u32[]{:S(2)}, u32[]{:S(2)}) %collective-permute-start.3) | collective-permute-done | bytes 147488 | tf_op jit(solution)/shard_map/ppermute | solution.py:23
  179.2 0.1 pad_maximum_fusion
  179.3 0.1 broadcast_in_dim.7
  179.4 0.1 slice.146
  179.5 2.3 %broadcast_in_dim.8 = bf16[2,6,96,2,384]{4,3,2,1,0:T(2,128)(2,1)} broadcast(bf16[2,6,96,384]{3,2,1,0:T(8,128)(2,1)S(1)} %slice.146), dimensions={0,1,2,4} | broadcast | bytes 2654208 | tf_op jit(solution)/shard_map/broadcast_in_dim | solution.py:97
  181.8 4.0 %reshape.92 = bf16[2,6,192,384]{3,2,1,0:T(8,128)(2,1)S(1)} reshape(bf16[2,6,96,2,384]{4,3,2,1,0:T(2,128)(2,1)} %broadcast_in_dim.8) | data formatting | bytes 3538944 | tf_op jit(solution)/shard_map/reshape | solution.py:97
  185.8 0.0 copy-start.3
  185.8 4.0 %pad_slice_fusion = (bf16[2,4,192,384]{3,2,1,0:T(8,128)(2,1)S(1)}, bf16[2,4,192,384]{3,2,1,0:T(8,128)(2,1)S(1)}, bf16[2,4,192,384]{3,2,1,0:T(8,128)(2,1)S(1)}, b...) fusion(bf16[2,6,192,384]{3,2,1,0:T(8,128)(2,1)S(1)} %reshape.92), kind=kLoop, calls=%fused_computation.34 | loop fusion | bytes 15925248 | tf_op jit(solution)/shard_map/slice | solution.py:103
  189.8 0.0 copy-done.3
  189.9 0.6 convolution_add_fusion.8
  190.4 0.6 convolution_add_fusion.7
  191.0 0.6 convolution_add_fusion.6
  191.6 0.6 convolution_add_fusion.5
  192.2 0.6 convolution_add_fusion.4
  192.8 0.6 convolution_add_fusion.3
  193.4 0.6 convolution_add_fusion.2
  193.9 0.6 convolution_add_fusion.1
  194.5 0.6 fusion.5
  195.1 1.2 copy.13
  (6 shorter events, 0.1 us)
Async XLA Ops:
  6.5 138.9 %copy-start = (bf16[384,384]{1,0:T(8,128)(2,1)S(1)}, bf16[384,384]{1,0:T(8,128)(2,1)}, u32[]{:S(2)}) copy-start(bf16[384,384]{1,0:T(8,128)(2,1)} %param.16) | copy-start | bytes 884740
  6.5 115.9 %all-gather.2.cloned.1.call-start = ((), (), s32[]{:S(2)}) async-start(), calls=%async_computation | async-start | bytes 4866048 | tf_op jit(solution)/shard_map/all_gather | solution.py:60
  137.0 8.4 %copy-start.1 = (bf16[1,2,96,384]{3,2,1,0:T(8,128)(2,1)S(1)}, bf16[1,2,96,384]{3,2,1,0:T(8,128)(2,1)}, u32[]{:S(2)}) copy-start(bf16[1,2,96,384]{3,2,1,0:T(8,128)(2,1)} %param.11) | copy-start | bytes 442372
  137.0 15.5 %copy-start.2 = (bf16[3,384,768]{2,1,0:T(8,128)(2,1)S(1)}, bf16[3,384,768]{2,1,0:T(8,128)(2,1)}, u32[]{:S(2)}) copy-start(bf16[3,384,768]{2,1,0:T(8,128)(2,1)} %param.18) | copy-start | bytes 5308420
  145.7 9.4 %collective-permute-start = (bf16[192,384]{1,0:T(8,128)(2,1)S(1)}, bf16[192,384]{1,0:T(8,128)(2,1)S(1)}, u32[]{:S(2)}, u32[]{:S(2)}) collective-permute-start(bf16[192,384]{1,0:T(8,128)(2,1)S(1)} %fusion.19), channel_id=1, source_target_pairs={{0,64},{32,96},{64,128},{96,160},{128,192},{160,224},{192,256},{22... | collective-permute-start | bytes 442376 | tf_op jit(solution)/shard_map/ppermute | solution.py:12
  150.3 8.9 %collective-permute-start.1 = (bf16[192,384]{1,0:T(8,128)(2,1)S(1)}, bf16[192,384]{1,0:T(8,128)(2,1)S(1)}, u32[]{:S(2)}, u32[]{:S(2)}) collective-permute-start(bf16[192,384]{1,0:T(8,128)(2,1)S(1)} %fusion.19), channel_id=1, source_target_pairs={{0,32},{32,64},{64,96},{96,128},{128,160},{160,192},{192,224},{224... | collective-permute-start | bytes 442376 | tf_op jit(solution)/shard_map/ppermute | solution.py:12
  159.5 9.3 %copy-start.4 = (bf16[192]{0:T(256)(128)(2,1)S(1)}, bf16[192]{0:T(256)(128)(2,1)}, u32[]{:S(2)}) copy-start(bf16[192]{0:T(256)(128)(2,1)} %param.21) | copy-start | bytes 1156
  159.9 10.5 %collective-permute-start.2 = (bf16[2,1,96,384]{3,2,1,0:T(8,128)(2,1)S(1)}, bf16[2,1,96,384]{3,2,1,0:T(8,128)(2,1)S(1)}, u32[]{:S(2)}, u32[]{:S(2)}) collective-permute-start(bf16[2,1,96,384]{3,2,1,0:T(8,128)(2,1)S(1)} %get-tuple-element.14), channel_id=1, source_target_pairs={{0,1},{1,2},{2,3},{3,4},{4,5},{5,6},{6,7},{7,8},{8,9},{9,10},{10,1... | collective-permute-start | bytes 442376 | tf_op jit(solution)/shard_map/ppermute | solution.py:20
  166.7 12.4 %collective-permute-start.3 = (bf16[2,1,96,384]{3,2,1,0:T(8,128)(2,1)S(1)}, bf16[2,1,96,384]{3,2,1,0:T(8,128)(2,1)S(1)}, u32[]{:S(2)}, u32[]{:S(2)}) collective-permute-start(bf16[2,1,96,384]{3,2,1,0:T(8,128)(2,1)S(1)} %get-tuple-element.15), channel_id=1, source_target_pairs={{1,0},{2,1},{3,2},{4,3},{5,4},{6,5},{7,6},{8,7},{9,8},{10,9},{11,1... | collective-permute-start | bytes 442376 | tf_op jit(solution)/shard_map/ppermute | solution.py:23
  185.8 4.1 %copy-start.3 = (bf16[3,3,384,192]{2,3,1,0:T(8,128)(2,1)S(1)}, bf16[3,3,384,192]{2,3,1,0:T(8,128)(2,1)}, u32[]{:S(2)}) copy-start(bf16[3,3,384,192]{2,3,1,0:T(8,128)(2,1)} %param.20) | copy-start | bytes 3981316
Sparse Core Ops, SparseCore 0:
  10.7 111.6 all-gather.1
where the time goes:
time: 204 us; the launch traced here: 203 us
  waiting for transfers between devices  125 us (61%)
  matrix products  24.1 us (12%)
  starting transfers between devices  15.7 us (8%)
  between operations  13.7 us (7%)
  local copies, waits for them, and re-layouts  12.8 us (6%)
  other arithmetic  11.6 us (6%)
    all_gather x1, waiting for transfers between devices, body(): lax.all_gather(frames.reshape(-1, channels), 'space', axis=0, tiled=True)  108 us
    ppermute x1, waiting for transfers between devices, with_halo(): lax.ppermute(lax.slice_in_dim(block, 0, width, axis=dim), axis, backward)  8.74 us
    dot_general x1, matrix products, attend(): jnp.dot(weights.astype(jnp.bfloat16), value_rows, preferred_element_type=...  8.41 us
    dot_general x1, matrix products, attend(): lax.dot_general(queries, key_rows, (((1,), (1,)), ((), ())), preferred_el...  8.06 us
    ppermute x2, starting transfers between devices, shifted(): lax.ppermute(value, axis, [(source, source + steps) for source in range(l...  6.8 us
    ppermute x1, starting transfers between devices, with_halo(): lax.ppermute(lax.slice_in_dim(block, block.shape[dim] - width, None, axis...  6.78 us
    ppermute x2, waiting for transfers between devices, shifted(): lax.ppermute(value, axis, [(source, source + steps) for source in range(l...  6.31 us
    dot_general x9, matrix products, body(): jnp.dot(window, w_space[row_tap, col_tap], preferred_element_type=jnp.flo...  5.18 us
  transfers between devices with their start and end apart: 5, of which 5 were waited for; matrix products, arithmetic and copies ran while one was open for 4% of the time, Pallas kernels for 0%

commit v1 on v0

--- a/solution.py
+++ b/solution.py
@@ -57,7 +57,11 @@
     channels = frames.shape[-1]
     rows = frames.shape[1]
     width = frames.shape[2]
-    whole = lax.all_gather(frames.reshape(-1, channels), "space", axis=0, tiled=True)
+    piece_in = frames.reshape(-1, channels)
+    res = jax.lax.psum(1, "space")
+    mid_arr = jnp.stack(res * [piece_in])
+    all_values = jax.lax.all_to_all(mid_arr, "space", 0, 0)
+    whole = jnp.concatenate(all_values, 0)
     normed = normalize(frames, norm_gain).reshape(-1, channels)
     queries = project(normed, w_qkv[:, :channels], b_qkv[:channels])
     count = queries.shape[0]

time: 204 us -> 275 us (1.35)
  the two profiles are of different devices: /device:TPU:49 before, /device:TPU:81 now
where the time goes in v1:
time: 275 us; the launch traced here: 274 us
  waiting for transfers between devices  176 us (64%)
  starting transfers between devices  48 us (17%)
  matrix products  22.9 us (8%)
  local copies, waits for them, and re-layouts  15.7 us (6%)
  other arithmetic  11.6 us (4%)
    all_to_all x1, waiting for transfers between devices, body(): all_values = jax.lax.all_to_all(mid_arr, 'space', 0, 0)  162 us
    ppermute x1, starting transfers between devices, with_halo(): lax.ppermute(lax.slice_in_dim(block, block.shape[dim] - width, None, axis...  25 us
    all_to_all x1, starting transfers between devices, body(): all_values = jax.lax.all_to_all(mid_arr, 'space', 0, 0)  14.1 us
    dot_general x1, matrix products, attend(): jnp.dot(weights.astype(jnp.bfloat16), value_rows, preferred_element_type=...  8.37 us
    ppermute x1, waiting for transfers between devices, with_halo(): lax.ppermute(lax.slice_in_dim(block, 0, width, axis=dim), axis, backward)  8.23 us
    dot_general x1, matrix products, attend(): lax.dot_general(queries, key_rows, (((1,), (1,)), ((), ())), preferred_el...  7.89 us
    ppermute x2, starting transfers between devices, shifted(): lax.ppermute(value, axis, [(source, source + steps) for source in range(l...  6.89 us
    ppermute x2, waiting for transfers between devices, shifted(): lax.ppermute(value, axis, [(source, source + steps) for source in range(l...  5.52 us
  transfers between devices with their start and end apart: 5, of which 4 were waited for; matrix products, arithmetic and copies ran while one was open for 0% of the time, Pallas kernels for 0%

profile of v1, /device:TPU:81, one launch (start us, length us, event | category | flops | bytes accessed | tf_op | source)
XLA Modules:
  0.0 274.2 jit_solution(8093830139731514485)
XLA Ops:
  0.0 0.0 copy-start
  0.0 3.8 %stack.12 = bf16[32,192,384]{2,1,0:T(8,128)(2,1)} broadcast(bf16[192,384]{1,0:T(8,128)(2,1)} %bitcast.92), dimensions={1,2} | broadcast | bytes 4866048 | tf_op jit(solution)/shard_map/stack | solution.py:62
  3.8 0.0 copy-start.7
  3.8 0.0 copy-start.8
  3.8 0.0 copy-start.6
  3.9 0.0 copy-start.1
  3.9 0.0 copy-start.5
  3.9 0.0 copy-start.4
  3.9 0.0 copy-start.9
  3.9 14.1 %all-to-all-start = ((bf16[32,192,384]{2,1,0:T(8,128)(2,1)}), bf16[32,192,384]{2,1,0:T(8,128)(2,1)}, u32[]{:S(2)}, u32[]{:S(2)}) async-start(bf16[32,192,384]{2,1,0:T(8,128)(2,1)} %stack.12), calls=%async_computation | async-start | bytes 9437184 | tf_op jit(solution)/shard_map/all_to_all | solution.py:63
  18.0 0.0 copy-done.7
  18.0 0.0 copy-done.8
  18.0 0.0 copy-done.6
  18.0 0.0 copy-done.1
  18.0 0.1 fusion.28
  18.2 0.0 copy-done.5
  18.2 0.1 fusion.30
  18.3 0.0 copy-done.4
  18.4 0.0 copy-done.9
  18.4 0.2 fusion.12
  18.6 161.8 %all-to-all-done = bf16[32,192,384]{2,1,0:T(8,128)(2,1)} async-done(((bf16[32,192,384]{2,1,0:T(8,128)(2,1)}), bf16[32,192,384]{2,1,0:T(8,128)(2,1)}, u32[]{:S(2)}, u32[]{:S(2)}) %all-to-all-start) | async-done | bytes 4718624 | tf_op jit(solution)/shard_map/all_to_all | solution.py:63
  180.5 3.5 %multiply_reduce_fusion = f32[32,192]{1,0:T(8,128)S(1)} fusion(bf16[32,192,384]{2,1,0:T(8,128)(2,1)} %all-to-all-done), kind=kLoop, calls=%fused_computation.5 | loop fusion | flops 7071744 | bytes 4743168 | tf_op jit(solution)/shard_map/reduce_sum | solution.py:30
  184.0 0.1 rsqrt.21
  184.1 4.5 %fusion.1 = bf16[6144,384]{1,0:T(8,128)(2,1)} fusion(f32[384]{0:T(512)S(1)} %convert_element_type.73, f32[6144]{0:T(1024)S(1)} %rsqrt.21, bf16[32,192,384]{2,1,0:T(8,128)(2,1)} %all-to-all-done), kind=kLoop, calls=%fused_computation.2 | loop fusion | flops 9437184 | bytes 9463296 | tf_op jit(solution)/shard_map/convert_element_type | solution.py:31
  188.6 7.9 %fusion.58 = (f32[192]{0:T(256)S(1)}, f32[192,6144]{1,0:T(8,128)}) fusion(bf16[192,384]{1,0:T(8,128)(2,1)S(1)} %fusion.12, bf16[6144,384]{1,0:T(8,128)(2,1)} %fusion.1, f32[384]{0:T(512)S(1)} %get-tuple-element.24, bf16[384,1152]{1,0:T(8,128)(2,1)S(1)} %copy-done.9), kind=kOutput, calls=%fused_computation.89 | convolution fusion | flops 2724986624 | bytes 9882368 | tf_op jit(solution)/shard_map/dot_general | solution.py:42
  196.5 3.1 %fusion.2 = f32[192]{0:T(256)S(1)} fusion(f32[192,6144]{1,0:T(8,128)} %get-tuple-element.26, f32[192]{0:T(256)S(1)} %broadcast_maximum_fusion), kind=kLoop, calls=%fused_computation.8 | loop fusion | flops 2359104 | bytes 4720128 | tf_op jit(solution)/shard_map/reduce_sum | solution.py:47
  199.6 0.0 copy-start.2
  199.6 8.4 %fusion.17 = bf16[192,384]{1,0:T(8,128)(2,1)S(1)} fusion(f32[192,6144]{1,0:T(8,128)} %get-tuple-element.26, f32[192]{0:T(256)S(1)} %broadcast_maximum_fusion, bf16[6144,384]{1,0:T(8,128)(2,1)} %fusion.1, f32[384]{0:T(512)S(1)} %get-tuple-element.22, bf16[384,1152]{1,0:T(8,128)(2,1)} %param.14, f32[192]{0:T(256)S(1)} %fusion.2), kind=kOutput, calls=%fused_computation.32 | convolution fusion | flops 2725134336 | bytes 9882624 | tf_op jit(solution)/shard_map/dot_general | solution.py:48
  208.0 0.0 copy-done
  208.0 0.2 fusion.13
  208.2 4.7 %collective-permute-start = (bf16[192,384]{1,0:T(8,128)(2,1)S(1)}, bf16[192,384]{1,0:T(8,128)(2,1)S(1)}, u32[]{:S(2)}, u32[]{:S(2)}) collective-permute-start(bf16[192,384]{1,0:T(8,128)(2,1)S(1)} %fusion.13), channel_id=1, source_target_pairs={{0,64},{32,96},{64,128},{96,160},{128,192},{160,224},{192,256},{22... | collective-permute-start | bytes 442376 | tf_op jit(solution)/shard_map/ppermute | solution.py:12
  212.9 2.2 collective-permute-start.1
  215.1 0.0 copy-done.2
  215.1 0.3 fusion.20
  215.4 1.1 collective-permute-done
  216.5 4.5 %collective-permute-done.1 = bf16[192,384]{1,0:T(8,128)(2,1)S(1)} collective-permute-done((bf16[192,384]{1,0:T(8,128)(2,1)S(1)}, bf16[192,384]{1,0:T(8,128)(2,1)S(1)}, u32[]{:S(2)}, u32[]{:S(2)}) %collective-permute-start.1) | collective-permute-done | bytes 147488 | tf_op jit(solution)/shard_map/ppermute | solution.py:12
  221.0 0.1 fusion.46
  221.0 0.3 fusion.22
  221.4 0.0 copy-start.10
  221.4 0.3 fusion.10
  221.8 25.0 %collective-permute-start.2 = (bf16[2,1,96,384]{3,2,1,0:T(8,128)(2,1)S(1)}, bf16[2,1,96,384]{3,2,1,0:T(8,128)(2,1)S(1)}, u32[]{:S(2)}, u32[]{:S(2)}) collective-permute-start(bf16[2,1,96,384]{3,2,1,0:T(8,128)(2,1)S(1)} %get-tuple-element.14), channel_id=1, source_target_pairs={{0,1},{1,2},{2,3},{3,4},{4,5},{5,6},{6,7},{7,8},{8,9},{9,10},{10,1... | collective-permute-start | bytes 442376 | tf_op jit(solution)/shard_map/ppermute | solution.py:20
  246.8 2.1 collective-permute-start.3
  248.9 0.0 copy-done.10
  248.9 0.0 collective-permute-done.2
  248.9 8.2 %collective-permute-done.3 = bf16[2,1,96,384]{3,2,1,0:T(8,128)(2,1)S(1)} collective-permute-done((bf16[2,1,96,384]{3,2,1,0:T(8,128)(2,1)S(1)}, bf16[2,1,96,384]{3,2,1,0:T(8,128)(2,1)S(1)}, u32[]{:S(2)}, u32[]{:S(2)}) %collective-permute-start.3) | collective-permute-done | bytes 147488 | tf_op jit(solution)/shard_map/ppermute | solution.py:23
  257.1 0.1 pad_maximum_fusion
  257.2 0.1 broadcast_in_dim.7
  257.4 0.1 slice.146
  257.4 2.3 broadcast_in_dim.8
  259.7 4.0 %reshape.105 = bf16[2,6,192,384]{3,2,1,0:T(8,128)(2,1)S(1)} reshape(bf16[2,6,96,2,384]{4,3,2,1,0:T(2,128)(2,1)} %broadcast_in_dim.8) | data formatting | bytes 3538944 | tf_op jit(solution)/shard_map/reshape | solution.py:101
  263.7 0.0 copy-start.3
  263.7 4.0 %pad_slice_fusion = (bf16[2,4,192,384]{3,2,1,0:T(8,128)(2,1)S(1)}, bf16[2,4,192,384]{3,2,1,0:T(8,128)(2,1)S(1)}, bf16[2,4,192,384]{3,2,1,0:T(8,128)(2,1)S(1)}, b...) fusion(bf16[2,6,192,384]{3,2,1,0:T(8,128)(2,1)S(1)} %reshape.105), kind=kLoop, calls=%fused_computation.33 | loop fusion | bytes 15925248 | tf_op jit(solution)/shard_map/slice | solution.py:107
  267.7 0.0 copy-done.3
  267.8 0.6 convolution_add_fusion.8
  268.3 0.6 convolution_add_fusion.7
  268.9 0.6 convolution_add_fusion.6
  269.5 0.6 convolution_add_fusion.5
  270.1 0.6 convolution_add_fusion.4
  270.7 0.6 convolution_add_fusion.3
  271.3 0.6 convolution_add_fusion.2
  271.8 0.6 convolution_add_fusion.1
  272.4 0.6 fusion.4
  273.0 1.2 copy.14
  (11 shorter events, 0.1 us)
Async XLA Ops:
  0.0 208.0 %copy-start = (bf16[384,384]{1,0:T(8,128)(2,1)S(1)}, bf16[384,384]{1,0:T(8,128)(2,1)}, u32[]{:S(2)}) copy-start(bf16[384,384]{1,0:T(8,128)(2,1)} %param.16) | copy-start | bytes 884740
  3.8 14.1 %copy-start.7 = (bf16[384]{0:T(512)(128)(2,1)S(1)}, bf16[384]{0:T(512)(128)(2,1)}, u32[]{:S(2)}) copy-start(bf16[384]{0:T(512)(128)(2,1)} %param.13) | copy-start | bytes 2308
  3.8 14.1 %copy-start.8 = (bf16[384]{0:T(512)(128)(2,1)S(1)}, bf16[384]{0:T(512)(128)(2,1)}, u32[]{:S(2)}) copy-start(bf16[384]{0:T(512)(128)(2,1)} %param.17) | copy-start | bytes 2308
  3.8 14.2 %copy-start.6 = (bf16[768]{0:T(1024)(128)(2,1)S(1)}, bf16[768]{0:T(1024)(128)(2,1)}, u32[]{:S(2)}) copy-start(bf16[768]{0:T(1024)(128)(2,1)} %param.19) | copy-start | bytes 4612
  3.9 14.2 %copy-start.1 = (bf16[1,2,96,384]{3,2,1,0:T(8,128)(2,1)S(1)}, bf16[1,2,96,384]{3,2,1,0:T(8,128)(2,1)}, u32[]{:S(2)}) copy-start(bf16[1,2,96,384]{3,2,1,0:T(8,128)(2,1)} %param.11) | copy-start | bytes 442372
  3.9 14.3 %copy-start.5 = (bf16[1152]{0:T(1024)(128)(2,1)S(1)}, bf16[1152]{0:T(1024)(128)(2,1)}, u32[]{:S(2)}) copy-start(bf16[1152]{0:T(1024)(128)(2,1)} %param.15) | copy-start | bytes 6916
  3.9 14.4 %copy-start.4 = (bf16[2,2,96,384]{3,2,1,0:T(8,128)(2,1)S(1)}, bf16[2,2,96,384]{3,2,1,0:T(8,128)(2,1)}, u32[]{:S(2)}) copy-start(bf16[2,2,96,384]{3,2,1,0:T(8,128)(2,1)} %param.12) | copy-start | bytes 884740
  3.9 14.5 %copy-start.9 = (bf16[384,1152]{1,0:T(8,128)(2,1)S(1)}, bf16[384,1152]{1,0:T(8,128)(2,1)}, u32[]{:S(2)}) copy-start(bf16[384,1152]{1,0:T(8,128)(2,1)} %param.14) | copy-start | bytes 2654212
  3.9 176.6 %all-to-all-start = ((bf16[32,192,384]{2,1,0:T(8,128)(2,1)}), bf16[32,192,384]{2,1,0:T(8,128)(2,1)}, u32[]{:S(2)}, u32[]{:S(2)}) async-start(bf16[32,192,384]{2,1,0:T(8,128)(2,1)} %stack.12), calls=%async_computation | async-start | bytes 9437184 | tf_op jit(solution)/shard_map/all_to_all | solution.py:63
  199.6 15.5 %copy-start.2 = (bf16[3,384,768]{2,1,0:T(8,128)(2,1)S(1)}, bf16[3,384,768]{2,1,0:T(8,128)(2,1)}, u32[]{:S(2)}) copy-start(bf16[3,384,768]{2,1,0:T(8,128)(2,1)} %param.18) | copy-start | bytes 5308420
  208.2 8.3 %collective-permute-start = (bf16[192,384]{1,0:T(8,128)(2,1)S(1)}, bf16[192,384]{1,0:T(8,128)(2,1)S(1)}, u32[]{:S(2)}, u32[]{:S(2)}) collective-permute-start(bf16[192,384]{1,0:T(8,128)(2,1)S(1)} %fusion.13), channel_id=1, source_target_pairs={{0,64},{32,96},{64,128},{96,160},{128,192},{160,224},{192,256},{22... | collective-permute-start | bytes 442376 | tf_op jit(solution)/shard_map/ppermute | solution.py:12
  212.9 8.1 %collective-permute-start.1 = (bf16[192,384]{1,0:T(8,128)(2,1)S(1)}, bf16[192,384]{1,0:T(8,128)(2,1)S(1)}, u32[]{:S(2)}, u32[]{:S(2)}) collective-permute-start(bf16[192,384]{1,0:T(8,128)(2,1)S(1)} %fusion.13), channel_id=1, source_target_pairs={{0,32},{32,64},{64,96},{96,128},{128,160},{160,192},{192,224},{224... | collective-permute-start | bytes 442376 | tf_op jit(solution)/shard_map/ppermute | solution.py:12
  221.4 27.5 %copy-start.10 = (bf16[192]{0:T(256)(128)(2,1)S(1)}, bf16[192]{0:T(256)(128)(2,1)}, u32[]{:S(2)}) copy-start(bf16[192]{0:T(256)(128)(2,1)} %param.21) | copy-start | bytes 1156
  221.8 27.1 %collective-permute-start.2 = (bf16[2,1,96,384]{3,2,1,0:T(8,128)(2,1)S(1)}, bf16[2,1,96,384]{3,2,1,0:T(8,128)(2,1)S(1)}, u32[]{:S(2)}, u32[]{:S(2)}) collective-permute-start(bf16[2,1,96,384]{3,2,1,0:T(8,128)(2,1)S(1)} %get-tuple-element.14), channel_id=1, source_target_pairs={{0,1},{1,2},{2,3},{3,4},{4,5},{5,6},{6,7},{7,8},{8,9},{9,10},{10,1... | collective-permute-start | bytes 442376 | tf_op jit(solution)/shard_map/ppermute | solution.py:20
  246.8 10.4 %collective-permute-start.3 = (bf16[2,1,96,384]{3,2,1,0:T(8,128)(2,1)S(1)}, bf16[2,1,96,384]{3,2,1,0:T(8,128)(2,1)S(1)}, u32[]{:S(2)}, u32[]{:S(2)}) collective-permute-start(bf16[2,1,96,384]{3,2,1,0:T(8,128)(2,1)S(1)} %get-tuple-element.15), channel_id=1, source_target_pairs={{1,0},{2,1},{3,2},{4,3},{5,4},{6,5},{7,6},{8,7},{9,8},{10,9},{11,1... | collective-permute-start | bytes 442376 | tf_op jit(solution)/shard_map/ppermute | solution.py:23
  263.7 4.0 %copy-start.3 = (bf16[3,3,384,192]{2,3,1,0:T(8,128)(2,1)S(1)}, bf16[3,3,384,192]{2,3,1,0:T(8,128)(2,1)}, u32[]{:S(2)}) copy-start(bf16[3,3,384,192]{2,3,1,0:T(8,128)(2,1)} %param.20) | copy-start | bytes 3981316
